TPU v7x, 128 devices: a whole 4x4x4 slice. The times are simulated.
128 devices in a mesh: fsdp: 16 (over x_hi, y, core), dp: 8 (over z, x_lo).
Axes of the slice: x: 4 (x_hi: 2, x_lo: 2; x = x_hi * 2 + x_lo), y: 4, z: 4, core: 2. Of those that a mesh axis runs over, the one named last changes fastest.
Arguments:
- hidden: bfloat16 [12288, 8192], P('fsdp', 'dp'), may hold values from -6 to 6
- combine_weight: float32 [12288], P('fsdp'), may hold values from 0.2 to 1
- down_weight: bfloat16 [4096, 2, 8192], P('fsdp', None, 'dp'), may hold values from -0.0625 to 0.0625
- cotangent: bfloat16 [12288, 4096], P('fsdp', 'dp'), may hold values from -6 to 6
- expert_rows: int32 [16, 2], P('fsdp'), may hold values from 1 to 640, as said below
- block_expert: int32 [96], P('fsdp'), may hold values from 0 to 1, as said below
- slot_token: int32 [12288], P('fsdp'), may hold values from 0 to 767, as said below
Outputs:
- expert_out: bfloat16 [12288, 4096], P('fsdp', 'dp')
- grad_hidden: bfloat16 [12288, 8192], P('fsdp', 'dp')
- grad_down: bfloat16 [4096, 2, 8192], P('fsdp', None, 'dp')
Inputs may be any that keep to these rules, and one draw needn't show every extreme that they name: `expert_rows`: row i gives the live rows of the first and the second expert in group i; the first expert's rows fill blocks from block 0 on, the second's start at the next free block, each takes ceil(rows / 128) blocks and both together at most 6; in every draw some group uses all 6 blocks. `block_expert`: within each group: 0 for the first expert's blocks, 1 for every later block; blocks past both experts' have no live rows. `slot_token`: tokens counted within the slot's group; the live slots of one expert in a group name different tokens of that group; slots that are not live hold arbitrary tokens.
All inputs are finite; a program needn't handle non-finite values.
Results may differ from a plain program's by a relative error of at most 0.014.
Values may be sent and summed in bfloat16 or wider, within the bound.
No kernel may reach another device: no remote copies, remote signals or barrier semaphores. Data moves between devices by JAX's collectives and lax.ppermute only.
A program may use at most 192 MiB of HBM per device.

v0:
```python
import math
import jax
import jax.numpy as jnp
from jax import lax
from jax.sharding import PartitionSpec as P

EXPERTS = 2
BLK = 128


def local(hidden, combine_weight, down_weight, cotangent, expert_rows, block_expert, slot_token):
    slot_count = hidden.shape[0]
    hidden_width = hidden.shape[1]
    block_count = block_expert.shape[0]
    positions = jnp.arange(slot_count, dtype=jnp.int32)
    blocks = positions // BLK
    live_rows = expert_rows[0]
    first_blocks = (live_rows[0] + BLK - 1) // BLK
    second_blocks = (live_rows[1] + BLK - 1) // BLK
    live = jnp.where(
        blocks < first_blocks,
        positions < live_rows[0],
        (blocks < first_blocks + second_blocks) & (positions - first_blocks * BLK < live_rows[1]),
    )
    slot_scale = combine_weight * live.astype(jnp.float32)
    full_cot = lax.all_gather(cotangent, "dp", axis=1, tiled=True)
    model_width = full_cot.shape[1]
    slot_cot = (slot_scale[:, None] * full_cot[slot_token].astype(jnp.float32)).astype(jnp.bfloat16)
    hid_blocks = hidden.reshape(block_count, BLK, hidden_width)
    cot_blocks = slot_cot.reshape(block_count, BLK, model_width)
    panel = lax.all_gather(down_weight, "fsdp", axis=0, tiled=True)
    extent = panel.shape[0]

    def per_block(carry, inputs):
        hid_block, cot_block, expert = inputs
        weight = lax.dynamic_index_in_dim(panel, expert, 1, keepdims=False)
        out_block = jnp.einsum("th,ch->tc", hid_block, weight, preferred_element_type=jnp.float32)
        grad_block = jnp.einsum("tc,ch->th", cot_block, weight, preferred_element_type=jnp.float32)
        return (carry, (out_block, grad_block))

    unused, (out_piece, grad_piece) = lax.scan(per_block, 0, (hid_blocks, cot_blocks, block_expert))
    slot_out = out_piece.reshape(slot_count, extent)
    slot_out, hidden_grad = (slot_out, grad_piece.reshape(slot_count, hidden_width))
    token_count = cotangent.shape[0]
    combined = (
        jnp.zeros((token_count, model_width), jnp.float32)
        .at[slot_token]
        .add(slot_scale[:, None] * slot_out)
    )
    expert_out = lax.psum_scatter(
        combined.astype(jnp.bfloat16), "dp", scatter_dimension=1, tiled=True
    )
    block_marks = (block_expert[:, None] == jnp.arange(EXPERTS, dtype=jnp.int32)[None, :]).astype(
        jnp.bfloat16
    )
    slot_marks = jnp.repeat(block_marks, BLK, axis=0)
    masked = slot_marks[:, :, None] * slot_cot[:, None, :]
    summed = lax.psum_scatter(
        jnp.einsum("sec,sh->ceh", masked, hidden, preferred_element_type=jnp.float32).astype(
            jnp.bfloat16
        ),
        "fsdp",
        scatter_dimension=0,
        tiled=True,
    ).astype(jnp.float32)
    grad_scale = 1.0 / math.sqrt(lax.axis_size("fsdp") * slot_count)
    grad_down = (summed * grad_scale).astype(jnp.bfloat16)
    return (expert_out, hidden_grad.astype(jnp.bfloat16), grad_down)


def solution(mesh):
    in_specs = (
        P("fsdp", "dp"),
        P("fsdp"),
        P("fsdp", None, "dp"),
        P("fsdp", "dp"),
        P("fsdp", None),
        P("fsdp"),
        P("fsdp"),
    )
    out_specs = (P("fsdp", "dp"), P("fsdp", "dp"), P("fsdp", None, "dp"))
    return jax.shard_map(local, mesh=mesh, in_specs=in_specs, out_specs=out_specs, check_vma=False)
```

profile of v0, /device:TPU:1, one launch (start us, length us, event | category | flops | bytes accessed | tf_op | source)
XLA Modules:
  0.0 673.4 jit_solution(6814083249735016535)
XLA Ops:
  18.3 123.9 %all-gather.5.cloned.1.call-done = bf16[768,4096]{1,0:T(8,128)(2,1)} async-done(((bf16[768,512]{1,0:T(8,128)(2,1)}), bf16[768,4096]{1,0:T(8,128)(2,1)}) %all-gather.5.cloned.1.call-update) | async-done | bytes 6291472 | tf_op jit(solution)/shard_map/all_gather | solution.py:26
  142.2 15.6 %gather_fusion = bf16[768,4096]{1,0:T(8,128)(2,1)} fusion(bf16[768,4096]{1,0:T(8,128)(2,1)} %all-gather.5.cloned.1.call-done, s32[1024]{0:T(1024)S(1)} %pad_clamp_fusion), kind=kCustom, calls=%fused_computation | custom fusion | bytes 12585984 | tf_op jit(solution)/shard_map/gather | solution.py:28
  157.8 8.0 %multiply_convert_fusion.1 = bf16[6,128,4096]{2,1,0:T(8,128)(2,1)} fusion(f32[6,128]{1,0:T(8,128)S(1)} %fusion.42, bf16[6,128,4096]{2,1,0:T(8,128)(2,1)} %bitcast.64), kind=kLoop, calls=%fused_computation.23 | loop fusion | flops 9437184 | bytes 12585984 | tf_op jit(solution)/shard_map/convert_element_type | solution.py:28
  165.7 89.9 %all-gather.3.cloned.1.call-done = bf16[4096,2,1024]{2,0,1:T(8,128)(2,1)} async-done(((bf16[256,2,1024]{2,0,1:T(8,128)(2,1)}), bf16[4096,2,1024]{2,0,1:T(8,128)(2,1)}) %all-gather.3.cloned.1.call-update) | async-done | bytes 16777232 | tf_op jit(solution)/shard_map/all_gather | solution.py:31
  255.6 94.9 %while.12 = (s32[]{:T(128)}, f32[6,128,4096]{2,1,0:T(8,128)}, bf16[6,128,1024]{2,1,0:T(8,128)(2,1)}, bf16[6,128,1024]{2,1,0:T(8,128)(2,1)S(1)}, s32[6]{0:T(128)S...) while((s32[]{:T(128)}, f32[6,128,4096]{2,1,0:T(8,128)}, ...), condition=%wide.region_1.2_spmd, body=%wide.region_0.1_spmd.sunk | while | flops 2147483648 | bytes 20711580 | solution.py:41
  258.2 7.6 %fusion.53 = f32[6,128,4096]{2,1,0:T(8,128)} fusion(f32[6,128,4096]{2,1,0:T(8,128)} %get-tuple-element.121, s32[]{:T(128)} %get-tuple-element.120, bf16[4096,2,1024]{2,0,1:T(8,128)(2,1)} %get-tuple-element.135, s32[]{:T(128)S(6)} %select_n.50, bf16[6,128,1024]{2,1,0:T(8,128)(2,1)S(1)} %get-tuple-element.133), kind=kOutput, calls=%fused_computation.9.clone.1 | convolution fusion | flops 1073741824 | bytes 10748932 | tf_op jit(solution)/shard_map/while/body/eval_jaxpr/th,ch->tc/dot_general | solution.py:37
  265.8 5.7 fusion.54
  274.0 7.6 %fusion.53 = f32[6,128,4096]{2,1,0:T(8,128)} fusion(f32[6,128,4096]{2,1,0:T(8,128)} %get-tuple-element.121, s32[]{:T(128)} %get-tuple-element.120, bf16[4096,2,1024]{2,0,1:T(8,128)(2,1)} %get-tuple-element.135, s32[]{:T(128)S(6)} %select_n.50, bf16[6,128,1024]{2,1,0:T(8,128)(2,1)S(1)} %get-tuple-element.133), kind=kOutput, calls=%fused_computation.9.clone.1 | convolution fusion | flops 1073741824 | bytes 10748932 | tf_op jit(solution)/shard_map/while/body/eval_jaxpr/th,ch->tc/dot_general | solution.py:37
  281.5 5.7 fusion.54
  289.8 7.6 %fusion.53 = f32[6,128,4096]{2,1,0:T(8,128)} fusion(f32[6,128,4096]{2,1,0:T(8,128)} %get-tuple-element.121, s32[]{:T(128)} %get-tuple-element.120, bf16[4096,2,1024]{2,0,1:T(8,128)(2,1)} %get-tuple-element.135, s32[]{:T(128)S(6)} %select_n.50, bf16[6,128,1024]{2,1,0:T(8,128)(2,1)S(1)} %get-tuple-element.133), kind=kOutput, calls=%fused_computation.9.clone.1 | convolution fusion | flops 1073741824 | bytes 10748932 | tf_op jit(solution)/shard_map/while/body/eval_jaxpr/th,ch->tc/dot_general | solution.py:37
  297.4 5.7 fusion.54
  305.6 7.6 %fusion.53 = f32[6,128,4096]{2,1,0:T(8,128)} fusion(f32[6,128,4096]{2,1,0:T(8,128)} %get-tuple-element.121, s32[]{:T(128)} %get-tuple-element.120, bf16[4096,2,1024]{2,0,1:T(8,128)(2,1)} %get-tuple-element.135, s32[]{:T(128)S(6)} %select_n.50, bf16[6,128,1024]{2,1,0:T(8,128)(2,1)S(1)} %get-tuple-element.133), kind=kOutput, calls=%fused_computation.9.clone.1 | convolution fusion | flops 1073741824 | bytes 10748932 | tf_op jit(solution)/shard_map/while/body/eval_jaxpr/th,ch->tc/dot_general | solution.py:37
  313.2 5.7 fusion.54
  321.4 7.6 %fusion.53 = f32[6,128,4096]{2,1,0:T(8,128)} fusion(f32[6,128,4096]{2,1,0:T(8,128)} %get-tuple-element.121, s32[]{:T(128)} %get-tuple-element.120, bf16[4096,2,1024]{2,0,1:T(8,128)(2,1)} %get-tuple-element.135, s32[]{:T(128)S(6)} %select_n.50, bf16[6,128,1024]{2,1,0:T(8,128)(2,1)S(1)} %get-tuple-element.133), kind=kOutput, calls=%fused_computation.9.clone.1 | convolution fusion | flops 1073741824 | bytes 10748932 | tf_op jit(solution)/shard_map/while/body/eval_jaxpr/th,ch->tc/dot_general | solution.py:37
  329.0 5.7 fusion.54
  337.2 7.6 %fusion.53 = f32[6,128,4096]{2,1,0:T(8,128)} fusion(f32[6,128,4096]{2,1,0:T(8,128)} %get-tuple-element.121, s32[]{:T(128)} %get-tuple-element.120, bf16[4096,2,1024]{2,0,1:T(8,128)(2,1)} %get-tuple-element.135, s32[]{:T(128)S(6)} %select_n.50, bf16[6,128,1024]{2,1,0:T(8,128)(2,1)S(1)} %get-tuple-element.133), kind=kOutput, calls=%fused_computation.9.clone.1 | convolution fusion | flops 1073741824 | bytes 10748932 | tf_op jit(solution)/shard_map/while/body/eval_jaxpr/th,ch->tc/dot_general | solution.py:37
  344.8 5.7 fusion.54
  350.5 14.9 %multiply_convert_fusion = (bf16[768,4096]{1,0:T(8,128)(2,1)}, f32[768,4096]{1,0:T(8,128)}) fusion(f32[768]{0:T(1024)S(1)} %fusion.38, bf16[768,4096]{1,0:T(8,128)(2,1)} %gather_fusion, f32[6,128,4096]{2,1,0:T(8,128)} %get-tuple-element.41), kind=kLoop, calls=%fused_computation.22 | loop fusion | flops 12582912 | bytes 37751808 | tf_op jit(solution)/shard_map/convert_element_type | solution.py:28
  365.5 8.7 %copy.13 = bf16[768,4096]{0,1:T(8,128)(2,1)} copy(bf16[768,4096]{1,0:T(8,128)(2,1)} %get-tuple-element.63) | data formatting | bytes 12582912 | tf_op jit(solution)/shard_map/convert_element_type | solution.py:28
  374.1 17.7 %convert_bitcast_fusion = bf16[4096,2,1024]{2,0,1:T(8,128)(2,1)} fusion(bf16[768,4096]{0,1:T(8,128)(2,1)} %copy.13, bf16[768,2]{0,1:T(2,128)(2,1)S(1)} %bitcast.65, bf16[768,1024]{1,0:T(8,128)(2,1)S(1)} %bitcast.67), kind=kOutput, calls=%fused_computation.18 | convolution fusion | flops 12899581952 | bytes 24644608 | tf_op jit(solution)/shard_map/sec,sh->ceh/dot_general | solution.py:59
  391.9 32.3 %scatter_custom_fusion = f32[768,4096]{1,0:T(8,128)} fusion(s32[768]{0:T(1024)S(1)} %compare_select_fusion, f32[768,4096]{1,0:T(8,128)} %get-tuple-element.64, f32[]{:T(128)} %constant.60.clone.1), kind=kCustom, calls=%fused_computation.26 | custom fusion | flops 3145728 | bytes 12583424 | tf_op jit(solution)/shard_map/scatter-add | solution.py:48
  424.2 8.4 %convert_element_type.51 = bf16[768,4096]{1,0:T(8,128)(2,1)} convert(f32[768,4096]{1,0:T(8,128)} %scatter_custom_fusion) | non-fusion elementwise | flops 3145728 | bytes 18874368 | tf_op jit(solution)/shard_map/convert_element_type | solution.py:51
  432.6 103.0 %reduce-scatter.5.cloned.1.call-done = bf16[256,2,1024]{2,0,1:T(8,128)(2,1)} async-done(((bf16[4096,2,1024]{2,0,1:T(8,128)(2,1)}), bf16[256,2,1024]{2,0,1:T(8,128)(2,1)}) %reduce-scatter.5.cloned.1.call-update) | async-done | bytes 1048592 | tf_op jit(solution)/shard_map/reduce_scatter | solution.py:58
  539.0 127.8 %reduce-scatter.3.cloned.1.call-done = bf16[768,512]{1,0:T(8,128)(2,1)} async-done(((bf16[768,4096]{1,0:T(8,128)(2,1)}), bf16[768,512]{1,0:T(8,128)(2,1)}) %reduce-scatter.3.cloned.1.call-update) | async-done | bytes 786448 | tf_op jit(solution)/shard_map/reduce_scatter | solution.py:50
  (31 shorter events, 16.8 us)
Async XLA Ops:
  7.2 135.0 %all-gather.5.cloned.1.call-start = ((), (), s32[]{:S(2)}) async-start(), calls=%async_computation.3 | async-start | bytes 7077888 | tf_op jit(solution)/shard_map/all_gather | solution.py:26
  7.9 247.7 %all-gather.3.cloned.1.call-start = ((), (), s32[]{:S(2)}) async-start(), calls=%async_computation.2 | async-start | bytes 17825792 | tf_op jit(solution)/shard_map/all_gather | solution.py:31
  10.4 525.1 %reduce-scatter.5.cloned.1.call-start = ((), (), s32[]{:S(2)}) async-start(), calls=%async_computation.5 | async-start | bytes 17825792 | tf_op jit(solution)/shard_map/reduce_scatter | solution.py:58
  157.8 97.9 %copy-start = (bf16[768,1024]{1,0:T(8,128)(2,1)S(1)}, bf16[768,1024]{1,0:T(8,128)(2,1)}, u32[]{:S(2)}) copy-start(bf16[768,1024]{1,0:T(8,128)(2,1)} %param.9) | copy-start | bytes 4718596
  157.8 97.9 %copy-start.1 = (s32[6]{0:T(128)S(1)}, s32[6]{0:T(128)}, u32[]{:S(2)}) copy-start(s32[6]{0:T(128)} %param.14) | copy-start | bytes 76
  391.9 275.0 %reduce-scatter.3.cloned.1.call-start = ((), (), s32[]{:S(2)}) async-start(), calls=%async_computation.4 | async-start | bytes 7077888 | tf_op jit(solution)/shard_map/reduce_scatter | solution.py:50
Sparse Core Ops, SparseCore 0:
  9.6 132.4 all-gather.4
  145.3 110.3 all-gather.2
  392.0 143.4 reduce-scatter.4
  538.4 128.4 reduce-scatter.2
where the time goes:
time: 674 us; the launch traced here: 673 us
  waiting for transfers between devices  445 us (66%)
  matrix products  97.4 us (14%)
  other arithmetic  70.1 us (10%)
  local copies, waits for them, and re-layouts  33.6 us (5%)
  between operations  15.1 us (2%)
  loops' own time  11.7 us (2%)
    reduce_scatter x1, waiting for transfers between devices, local(): lax.psum_scatter(combined.astype(jnp.bfloat16), 'dp', scatter_dimension=1...  128 us
    all_gather x1, waiting for transfers between devices, local(): full_cot = lax.all_gather(cotangent, 'dp', axis=1, tiled=True)  124 us
    reduce_scatter x1, waiting for transfers between devices, local(): lax.psum_scatter(jnp.einsum('sec,sh->ceh', masked, hidden, preferred_elem...  103 us
    all_gather x1, waiting for transfers between devices, local(): panel = lax.all_gather(down_weight, 'fsdp', axis=0, tiled=True)  89.9 us
    dot_general x6, matrix products, per_block(): jnp.einsum('th,ch->tc', hid_block, weight, preferred_element_type=jnp.flo...  45.6 us
    dot_general x6, matrix products, per_block(): jnp.einsum('tc,ch->th', cot_block, weight, preferred_element_type=jnp.flo...  34.1 us
    scatter-add x1, other arithmetic, local(): combined = jnp.zeros((token_count, model_width), jnp.float32).at[slot_tok...  32.3 us
    convert_element_type x2, other arithmetic, local(): (slot_scale[:, None] * full_cot[slot_token].astype(jnp.float32)).astype(j...  22.9 us
  transfers between devices with their start and end apart: 4, of which 4 were waited for; matrix products, arithmetic and copies ran while one was open for 11% of the time, Pallas kernels for 0%

commit v1 on v0

--- a/solution.py
+++ b/solution.py
@@ -6,6 +6,12 @@
 
 EXPERTS = 2
 BLK = 128
+
+
+def test_view(w_in):
+    w1 = jnp.stack([w_in for _ in range(lax.psum(1, "dp"))])
+    piece_next = lax.all_to_all(w1, "dp", 0, 0)
+    return jnp.concatenate(piece_next, axis=1)
 
 
 def local(hidden, combine_weight, down_weight, cotangent, expert_rows, block_expert, slot_token):
@@ -23,7 +29,7 @@
         (blocks < first_blocks + second_blocks) & (positions - first_blocks * BLK < live_rows[1]),
     )
     slot_scale = combine_weight * live.astype(jnp.float32)
-    full_cot = lax.all_gather(cotangent, "dp", axis=1, tiled=True)
+    full_cot = test_view(cotangent)
     model_width = full_cot.shape[1]
     slot_cot = (slot_scale[:, None] * full_cot[slot_token].astype(jnp.float32)).astype(jnp.bfloat16)
     hid_blocks = hidden.reshape(block_count, BLK, hidden_width)

time: 674 us -> 588 us (0.87)
  waiting for transfers between devices: 445 us -> 345 us
  local copies, waits for them, and re-layouts: 33.6 us -> 43.5 us
  starting transfers between devices: 0.16 us -> 6.91 us
    all_gather x1 -> x0, waiting for transfers between devices: 124 us -> none  [local(): full_cot = lax.all_gather(cotangent, 'dp', axis=1, tiled=True)]
    all_to_all x0 -> x1, waiting for transfers between devices: none -> 107 us  [test_view(): piece_next = lax.all_to_all(w1, 'dp', 0, 0)]
    all_gather x1, waiting for transfers between devices: 89.9 us -> 4.23 us  [local(): panel = lax.all_gather(down_weight, 'fsdp', axis=0, tiled=True)]
    all_to_all x0 -> x1, starting transfers between devices: none -> 6.79 us  [test_view(): piece_next = lax.all_to_all(w1, 'dp', 0, 0)]
  transfers between devices with their start and end apart: 4 -> 4, of which waited for: 4 -> 4; matrix products, arithmetic and copies ran while one was open for 11% -> 14% of each run, Pallas kernels for 0% -> 0%
where the time goes in v1:
time: 588 us; the launch traced here: 587 us
  waiting for transfers between devices  345 us (59%)
  matrix products  97.3 us (17%)
  other arithmetic  67.6 us (11%)
  local copies, waits for them, and re-layouts  43.5 us (7%)
  between operations  15.2 us (3%)
  loops' own time  11.7 us (2%)
  starting transfers between devices  6.91 us (1%)
    reduce_scatter x1, waiting for transfers between devices, local(): lax.psum_scatter(combined.astype(jnp.bfloat16), 'dp', scatter_dimension=1...  128 us
    all_to_all x1, waiting for transfers between devices, test_view(): piece_next = lax.all_to_all(w1, 'dp', 0, 0)  107 us
    reduce_scatter x1, waiting for transfers between devices, local(): lax.psum_scatter(jnp.einsum('sec,sh->ceh', masked, hidden, preferred_elem...  105 us
    dot_general x6, matrix products, per_block(): jnp.einsum('th,ch->tc', hid_block, weight, preferred_element_type=jnp.flo...  45.5 us
    dot_general x6, matrix products, per_block(): jnp.einsum('tc,ch->th', cot_block, weight, preferred_element_type=jnp.flo...  34.1 us
    scatter-add x1, other arithmetic, local(): combined = jnp.zeros((token_count, model_width), jnp.float32).at[slot_tok...  32.6 us
    convert_element_type x2, other arithmetic, local(): (slot_scale[:, None] * full_cot[slot_token].astype(jnp.float32)).astype(j...  22.8 us
    dot_general x1, matrix products, local(): jnp.einsum('sec,sh->ceh', masked, hidden, preferred_element_type=jnp.floa...  17.7 us
  transfers between devices with their start and end apart: 4, of which 4 were waited for; matrix products, arithmetic and copies ran while one was open for 14% of the time, Pallas kernels for 0%

profile of v1, /device:TPU:1, one launch (start us, length us, event | category | flops | bytes accessed | tf_op | source)
XLA Modules:
  0.0 587.0 jit_solution(4173383082600168386)
XLA Ops:
  14.0 6.8 %all-to-all-start = ((bf16[8,768,512]{2,1,0:T(8,128)(2,1)}), bf16[8,768,512]{2,1,0:T(8,128)(2,1)}, u32[]{:S(2)}, u32[]{:S(2)}) async-start(bf16[8,768,512]{2,1,0:T(8,128)(2,1)} %stack.2), calls=%async_computation | async-start | bytes 12582912 | tf_op jit(solution)/shard_map/all_to_all | solution.py:13
  25.6 107.0 %all-to-all-done = bf16[8,768,512]{2,1,0:T(8,128)(2,1)} async-done(((bf16[8,768,512]{2,1,0:T(8,128)(2,1)}), bf16[8,768,512]{2,1,0:T(8,128)(2,1)}, u32[]{:S(2)}, u32[]{:S(2)}) %all-to-all-start) | async-done | bytes 6291488 | tf_op jit(solution)/shard_map/all_to_all | solution.py:13
  132.6 6.3 %copy.19 = bf16[8,96,8,512]{3,2,0,1:T(8,128)(2,1)} copy(bf16[8,96,8,512]{3,2,1,0:T(8,128)(2,1)} %bitcast.16) | data formatting | bytes 12582912 | tf_op jit(solution)/shard_map/reshape | solution.py:14
  138.9 15.6 %gather_fusion = bf16[768,4096]{1,0:T(8,128)(2,1)} fusion(bf16[768,4096]{1,0:T(8,128)(2,1)} %bitcast.67, s32[1024]{0:T(1024)S(1)} %pad_clamp_fusion), kind=kCustom, calls=%fused_computation | custom fusion | bytes 12585984 | tf_op jit(solution)/shard_map/gather | solution.py:34
  154.5 8.1 %multiply_convert_fusion.1 = bf16[6,128,4096]{2,1,0:T(8,128)(2,1)} fusion(f32[6,128]{1,0:T(8,128)S(1)} %fusion.42, bf16[6,128,4096]{2,1,0:T(8,128)(2,1)} %bitcast.68), kind=kLoop, calls=%fused_computation.23 | loop fusion | flops 9437184 | bytes 12585984 | tf_op jit(solution)/shard_map/convert_element_type | solution.py:34
  166.8 94.7 %while.12 = (s32[]{:T(128)}, f32[6,128,4096]{2,1,0:T(8,128)}, bf16[6,128,1024]{2,1,0:T(8,128)(2,1)}, bf16[6,128,1024]{2,1,0:T(8,128)(2,1)S(1)}, s32[6]{0:T(128)S...) while((s32[]{:T(128)}, f32[6,128,4096]{2,1,0:T(8,128)}, ...), condition=%wide.region_1.2_spmd, body=%wide.region_0.1_spmd.sunk | while | flops 2147483648 | bytes 20711580 | solution.py:47
  169.3 7.6 %fusion.53 = f32[6,128,4096]{2,1,0:T(8,128)} fusion(f32[6,128,4096]{2,1,0:T(8,128)} %get-tuple-element.124, s32[]{:T(128)} %get-tuple-element.123, bf16[4096,2,1024]{2,0,1:T(8,128)(2,1)} %get-tuple-element.138, s32[]{:T(128)S(6)} %select_n.50, bf16[6,128,1024]{2,1,0:T(8,128)(2,1)S(1)} %get-tuple-element.136), kind=kOutput, calls=%fused_computation.9.clone.1 | convolution fusion | flops 1073741824 | bytes 10748932 | tf_op jit(solution)/shard_map/while/body/eval_jaxpr/th,ch->tc/dot_general | solution.py:43
  176.9 5.7 fusion.54
  185.1 7.6 %fusion.53 = f32[6,128,4096]{2,1,0:T(8,128)} fusion(f32[6,128,4096]{2,1,0:T(8,128)} %get-tuple-element.124, s32[]{:T(128)} %get-tuple-element.123, bf16[4096,2,1024]{2,0,1:T(8,128)(2,1)} %get-tuple-element.138, s32[]{:T(128)S(6)} %select_n.50, bf16[6,128,1024]{2,1,0:T(8,128)(2,1)S(1)} %get-tuple-element.136), kind=kOutput, calls=%fused_computation.9.clone.1 | convolution fusion | flops 1073741824 | bytes 10748932 | tf_op jit(solution)/shard_map/while/body/eval_jaxpr/th,ch->tc/dot_general | solution.py:43
  200.8 7.6 %fusion.53 = f32[6,128,4096]{2,1,0:T(8,128)} fusion(f32[6,128,4096]{2,1,0:T(8,128)} %get-tuple-element.124, s32[]{:T(128)} %get-tuple-element.123, bf16[4096,2,1024]{2,0,1:T(8,128)(2,1)} %get-tuple-element.138, s32[]{:T(128)S(6)} %select_n.50, bf16[6,128,1024]{2,1,0:T(8,128)(2,1)S(1)} %get-tuple-element.136), kind=kOutput, calls=%fused_computation.9.clone.1 | convolution fusion | flops 1073741824 | bytes 10748932 | tf_op jit(solution)/shard_map/while/body/eval_jaxpr/th,ch->tc/dot_general | solution.py:43
  208.4 5.7 fusion.54
  216.6 7.6 %fusion.53 = f32[6,128,4096]{2,1,0:T(8,128)} fusion(f32[6,128,4096]{2,1,0:T(8,128)} %get-tuple-element.124, s32[]{:T(128)} %get-tuple-element.123, bf16[4096,2,1024]{2,0,1:T(8,128)(2,1)} %get-tuple-element.138, s32[]{:T(128)S(6)} %select_n.50, bf16[6,128,1024]{2,1,0:T(8,128)(2,1)S(1)} %get-tuple-element.136), kind=kOutput, calls=%fused_computation.9.clone.1 | convolution fusion | flops 1073741824 | bytes 10748932 | tf_op jit(solution)/shard_map/while/body/eval_jaxpr/th,ch->tc/dot_general | solution.py:43
  224.2 5.7 fusion.54
  232.4 7.6 %fusion.53 = f32[6,128,4096]{2,1,0:T(8,128)} fusion(f32[6,128,4096]{2,1,0:T(8,128)} %get-tuple-element.124, s32[]{:T(128)} %get-tuple-element.123, bf16[4096,2,1024]{2,0,1:T(8,128)(2,1)} %get-tuple-element.138, s32[]{:T(128)S(6)} %select_n.50, bf16[6,128,1024]{2,1,0:T(8,128)(2,1)S(1)} %get-tuple-element.136), kind=kOutput, calls=%fused_computation.9.clone.1 | convolution fusion | flops 1073741824 | bytes 10748932 | tf_op jit(solution)/shard_map/while/body/eval_jaxpr/th,ch->tc/dot_general | solution.py:43
  240.0 5.7 fusion.54
  248.2 7.6 %fusion.53 = f32[6,128,4096]{2,1,0:T(8,128)} fusion(f32[6,128,4096]{2,1,0:T(8,128)} %get-tuple-element.124, s32[]{:T(128)} %get-tuple-element.123, bf16[4096,2,1024]{2,0,1:T(8,128)(2,1)} %get-tuple-element.138, s32[]{:T(128)S(6)} %select_n.50, bf16[6,128,1024]{2,1,0:T(8,128)(2,1)S(1)} %get-tuple-element.136), kind=kOutput, calls=%fused_computation.9.clone.1 | convolution fusion | flops 1073741824 | bytes 10748932 | tf_op jit(solution)/shard_map/while/body/eval_jaxpr/th,ch->tc/dot_general | solution.py:43
  255.8 5.7 fusion.54
  261.5 14.8 %multiply_convert_fusion = (bf16[768,4096]{1,0:T(8,128)(2,1)}, f32[768,4096]{1,0:T(8,128)}) fusion(f32[768]{0:T(1024)S(1)} %fusion.38, bf16[768,4096]{1,0:T(8,128)(2,1)} %gather_fusion, f32[6,128,4096]{2,1,0:T(8,128)} %get-tuple-element.41), kind=kLoop, calls=%fused_computation.22 | loop fusion | flops 12582912 | bytes 37751808 | tf_op jit(solution)/shard_map/convert_element_type | solution.py:34
  276.2 8.6 %copy.17 = bf16[768,4096]{0,1:T(8,128)(2,1)} copy(bf16[768,4096]{1,0:T(8,128)(2,1)} %get-tuple-element.66) | data formatting | bytes 12582912 | tf_op jit(solution)/shard_map/convert_element_type | solution.py:34
  284.9 17.7 %convert_bitcast_fusion = bf16[4096,2,1024]{2,0,1:T(8,128)(2,1)} fusion(bf16[768,4096]{0,1:T(8,128)(2,1)} %copy.17, bf16[768,2]{0,1:T(2,128)(2,1)S(1)} %bitcast.69, bf16[768,1024]{1,0:T(8,128)(2,1)S(1)} %bitcast.71), kind=kOutput, calls=%fused_computation.18 | convolution fusion | flops 12899581952 | bytes 24644608 | tf_op jit(solution)/shard_map/sec,sh->ceh/dot_general | solution.py:65
  302.7 32.6 %scatter_custom_fusion = f32[768,4096]{1,0:T(8,128)} fusion(s32[768]{0:T(1024)S(1)} %compare_select_fusion, f32[768,4096]{1,0:T(8,128)} %get-tuple-element.67, f32[]{:T(128)} %constant.60.clone.1), kind=kCustom, calls=%fused_computation.26 | custom fusion | flops 3145728 | bytes 12583424 | tf_op jit(solution)/shard_map/scatter-add | solution.py:54
  335.3 8.2 %convert_element_type.51 = bf16[768,4096]{1,0:T(8,128)(2,1)} convert(f32[768,4096]{1,0:T(8,128)} %scatter_custom_fusion) | non-fusion elementwise | flops 3145728 | bytes 18874368 | tf_op jit(solution)/shard_map/convert_element_type | solution.py:57
  343.5 105.4 %reduce-scatter.5.cloned.1.call-done = bf16[256,2,1024]{2,0,1:T(8,128)(2,1)} async-done(((bf16[4096,2,1024]{2,0,1:T(8,128)(2,1)}), bf16[256,2,1024]{2,0,1:T(8,128)(2,1)}) %reduce-scatter.5.cloned.1.call-update) | async-done | bytes 1048592 | tf_op jit(solution)/shard_map/reduce_scatter | solution.py:64
  452.4 128.0 %reduce-scatter.3.cloned.1.call-done = bf16[768,512]{1,0:T(8,128)(2,1)} async-done(((bf16[768,4096]{1,0:T(8,128)(2,1)}), bf16[768,512]{1,0:T(8,128)(2,1)}) %reduce-scatter.3.cloned.1.call-update) | async-done | bytes 786448 | tf_op jit(solution)/shard_map/reduce_scatter | solution.py:56
  (38 shorter events, 27.1 us)
Async XLA Ops:
  7.2 159.6 %all-gather.2.cloned.1.call-start = ((), (), s32[]{:S(2)}) async-start(), calls=%async_computation.3 | async-start | bytes 17825792 | tf_op jit(solution)/shard_map/all_gather | solution.py:37
  9.7 11.2 %copy-start.2 = (s32[1,2]{1,0:T(1,128)S(1)}, s32[1,2]{1,0:T(1,128)}, u32[]{:S(2)}) copy-start(s32[1,2]{1,0:T(1,128)} %param.13) | copy-start | bytes 28
  9.7 13.1 %copy-start.4 = (s32[6]{0:T(128)S(1)}, s32[6]{0:T(128)}, u32[]{:S(2)}) copy-start(s32[6]{0:T(128)} %param.14) | copy-start | bytes 76
  9.7 13.2 %copy-start.1 = (s32[768]{0:T(1024)S(1)}, s32[768]{0:T(1024)}, u32[]{:S(2)}) copy-start(s32[768]{0:T(1024)} %param.15) | copy-start | bytes 9220
  9.7 13.2 %copy-start = (f32[768]{0:T(1024)S(1)}, f32[768]{0:T(1024)}, u32[]{:S(2)}) copy-start(f32[768]{0:T(1024)} %param.10) | copy-start | bytes 9220
  14.0 118.6 %all-to-all-start = ((bf16[8,768,512]{2,1,0:T(8,128)(2,1)}), bf16[8,768,512]{2,1,0:T(8,128)(2,1)}, u32[]{:S(2)}, u32[]{:S(2)}) async-start(bf16[8,768,512]{2,1,0:T(8,128)(2,1)} %stack.2), calls=%async_computation | async-start | bytes 12582912 | tf_op jit(solution)/shard_map/all_to_all | solution.py:13
  20.8 428.1 %reduce-scatter.5.cloned.1.call-start = ((), (), s32[]{:S(2)}) async-start(), calls=%async_computation.5 | async-start | bytes 17825792 | tf_op jit(solution)/shard_map/reduce_scatter | solution.py:64
  154.5 12.3 %copy-start.3 = (bf16[768,1024]{1,0:T(8,128)(2,1)S(1)}, bf16[768,1024]{1,0:T(8,128)(2,1)}, u32[]{:S(2)}) copy-start(bf16[768,1024]{1,0:T(8,128)(2,1)} %param.9) | copy-start | bytes 4718596
  302.6 277.8 %reduce-scatter.3.cloned.1.call-start = ((), (), s32[]{:S(2)}) async-start(), calls=%async_computation.4 | async-start | bytes 7077888 | tf_op jit(solution)/shard_map/reduce_scatter | solution.py:56
Sparse Core Ops, SparseCore 0:
  11.1 155.6 all-gather.1
  302.8 146.0 reduce-scatter.4
  451.9 128.4 reduce-scatter.2
